TPU v7x, 256 devices: a whole 4x4x8 slice. The times are simulated.
256 devices in a mesh: shard: 64 (over y, z, core), cent: 4 (over x).
Axes of the slice: x: 4, y: 4, z: 8, core: 2. Of those that a mesh axis runs over, the one named last changes fastest.
Arguments:
- queries: bfloat16 [1024, 32, 128], P('shard'), may hold values from -6 to 6
- centroids: bfloat16 [196608, 128], P(('shard', 'cent')), may hold values from -0.5 to 0.5
- passages: bfloat16 [16384, 128, 128], P('shard', 'cent'), may hold values from -0.5 to 0.5
- lengths: int32 [16384], P('shard'), may hold values from 16 to 128, as said below
- passage_row: int32 [16384], replicated, may hold values from 0 to 16383, as said below
- candidates: int32 [1024, 16], P('shard'), may hold values from 0 to 16383, as said below
Outputs:
- token_best: float32 [1024, 32], P('shard')
- scores: float32 [1024, 16], P('shard')
Inputs may be any that keep to these rules, and one draw needn't show every extreme that they name: A permutation: passage g is stored at row passage_row[g]. The rows j < lengths[r] of stored passage r are real, the rest padding; the first stored passage of every index of shard has all 128. Among the 256 pairs of the queries of one index of shard, at most 12 have candidates stored at one owner (owner = passage_row[id] // 256); one owner takes exactly 12 pairs from every index of shard.
All inputs are finite; a program needn't handle non-finite values.
Results may differ from a plain program's by a relative error of at most 0.0003.
Values may be sent and summed in bfloat16 or wider, within the bound.
No kernel may reach another device: no remote copies, remote signals or barrier semaphores. Data moves between devices by JAX's collectives and lax.ppermute only.
A program may use at most 128 MiB of HBM per device.

v0:
```python
import jax
import jax.numpy as jnp
from jax import lax
from jax.sharding import PartitionSpec as P

masked_score = -1e30


def per_device(queries, centroids, passages, lengths, passage_row, candidates):
    query_count = queries.shape[0]
    query_tokens = queries.shape[1]
    feature_width = queries.shape[2]
    per_query = candidates.shape[1]
    passage_count = passages.shape[0]
    token_rows = passages.shape[1]
    shard_total = lax.axis_size("shard")
    capacity = max(2, 3 * query_count * per_query // shard_total)
    pairs_here = query_count * per_query
    my_shard = lax.axis_index("shard")
    query_block = lax.all_gather(queries, "shard", axis=0, tiled=True)
    cand_block = lax.all_gather(candidates, "shard", axis=0, tiled=True)
    flattened = query_block.reshape(-1, feature_width)
    scored = jnp.einsum("rd,cd->rc", flattened, centroids, preferred_element_type=jnp.float32)
    local_best = jnp.max(scored, axis=1).reshape(shard_total, query_count, query_tokens)
    gathered_best = lax.all_to_all(local_best, "shard", split_axis=0, concat_axis=0, tiled=True)
    shard_best = jnp.max(gathered_best, axis=0)
    all_rows = jnp.take(passage_row, cand_block.reshape(-1), axis=0)
    is_mine = (all_rows // passage_count == my_shard).reshape(shard_total, pairs_here)
    mine_int = is_mine.astype(jnp.int32)
    rank = jnp.cumsum(mine_int, axis=1) - mine_int
    source_ids = jnp.arange(shard_total, dtype=jnp.int32)[:, None]
    places = jnp.where(is_mine, source_ids * capacity + rank, shard_total * capacity).reshape(-1)
    pair_query = jnp.arange(shard_total * pairs_here, dtype=jnp.int32) // per_query
    slot_table = (
        jnp.zeros((shard_total * capacity,), jnp.int32)
        .at[places]
        .set(all_rows % passage_count, mode="drop")
    )
    query_table = (
        jnp.zeros((shard_total * capacity,), jnp.int32).at[places].set(pair_query, mode="drop")
    )
    asked = jnp.take(query_block, query_table, axis=0)
    chosen = jnp.take(passages, slot_table, axis=0)
    pair_scored = jnp.einsum("ntd,npd->ntp", asked, chosen, preferred_element_type=jnp.float32)
    token_index = lax.axis_index("cent") * token_rows + jnp.arange(token_rows, dtype=jnp.int32)
    valid_tokens = token_index[None, :] < jnp.take(lengths, slot_table, axis=0)[:, None]
    pair_scored = jnp.where(valid_tokens[:, None, :], pair_scored, masked_score)
    partial_value = jnp.max(pair_scored, axis=2)
    merged = lax.pmax(jnp.concatenate([shard_best, partial_value], axis=0), "cent")
    token_best = merged[:query_count]
    complete = merged[query_count:]
    pair_scores = (jnp.sum(complete, axis=1) / query_tokens).reshape(shard_total, capacity)
    returned = lax.all_to_all(pair_scores, "shard", split_axis=0, concat_axis=0, tiled=True)
    pair_rows = jnp.take(passage_row, candidates.reshape(-1), axis=0)
    owners = pair_rows // passage_count
    onehot = (owners[:, None] == jnp.arange(shard_total, dtype=jnp.int32)[None, :]).astype(
        jnp.int32
    )
    ranking = jnp.sum((jnp.cumsum(onehot, axis=0) - onehot) * onehot, axis=1)
    my_places = owners * capacity + ranking
    scores = jnp.take(returned.reshape(-1), my_places, axis=0).reshape(query_count, per_query)
    return (token_best, scores)


def solution(mesh):
    in_specs = (
        P("shard", None, None),
        P(("shard", "cent"), None),
        P("shard", "cent", None),
        P("shard"),
        P(),
        P("shard", None),
    )
    out_specs = (P("shard", None), P("shard", None))
    return jax.shard_map(
        per_device, mesh=mesh, in_specs=in_specs, out_specs=out_specs, check_vma=False
    )
```

profile of v0, /device:TPU:1, one launch (start us, length us, event | category | flops | bytes accessed | tf_op | source)
XLA Modules:
  0.0 415.2 jit_solution(12105765791642082866)
XLA Ops:
  7.2 0.0 copy-start
  7.2 0.0 copy-start.1
  7.2 0.0 all-gather.2.cloned.1.call-start
  7.2 0.7 all-gather.2.cloned.1.call-update
  7.9 0.8 reshape.445
  8.7 0.8 reshape.447
  9.5 0.8 reshape.446
  10.3 55.1 %all_gather.7 = s32[1024,16]{1,0:T(8,128)S(1)} all-gather(s32[16,16]{1,0:T(8,128)} %param.11), channel_id=1, replica_groups=mesh['shard'=64,'cent'=4] {'shard'}, dimensions={0}, use_global_device_ids=true | all-gather | bytes 66560 | tf_op jit(solution)/shard_map/all_gather | solution.py:21
  65.3 0.2 reshape.441
  65.6 0.2 reshape.444
  65.8 0.2 reshape.442
  66.0 2.1 gather_fusion.4
  68.1 0.6 reduce-window.16
  68.8 0.2 slice_reduce_fusion.1
  69.0 0.1 broadcast_bitcast_fusion
  69.1 0.1 copy.37
  69.1 0.1 compare_select_fusion.1
  69.2 0.0 copy-start.2
  69.3 90.5 %gather_fusion = s32[16384]{0:T(1024)S(1)} fusion(s32[16384]{0:T(1024)S(1)} %copy-done.1, s32[16384]{0:T(1024)S(1)} %broadcast_clamp_fusion), kind=kCustom, calls=%fused_computation | custom fusion | bytes 196608 | tf_op jit(solution)/shard_map/jit(_take)/gather | solution.py:27
  159.8 0.1 fusion.23
  159.9 0.6 reduce-window.14
  160.5 0.2 slice_reduce_fusion.2
  160.7 0.1 broadcast_add_fusion
  160.8 0.1 copy.30
  160.9 0.5 compare_select_fusion
  161.5 60.3 %scatter_custom_fusion.1 = s32[768]{0:T(1024)S(1)} fusion(s32[16384]{0:T(1024)S(1)} %bitcast.49, s32[16384]{0:T(1024)S(1)} %add_select_fusion, s32[]{:T(128)} %constant.143.clone.1), kind=kCustom, calls=%fused_computation.97 | custom fusion | bytes 3076 | tf_op jit(solution)/shard_map/scatter | solution.py:40
  221.8 60.5 %scatter_custom_fusion = s32[768]{0:T(1024)S(1)} fusion(s32[16384]{0:T(1024)S(1)} %bitcast.50, s32[16384]{0:T(1024)S(1)} %add_select_fusion.1, s32[]{:T(128)} %constant.143.clone.1), kind=kCustom, calls=%fused_computation.99 | custom fusion | bytes 3076 | tf_op jit(solution)/shard_map/scatter | solution.py:37
  282.3 5.0 %gather_fusion.1 = s32[768]{0:T(1024)S(1)} fusion(s32[256]{0:T(256)S(1)} %copy-done.2, s32[1024]{0:T(1024)S(1)} %pad_clamp_fusion.3), kind=kCustom, calls=%fused_computation.1 | custom fusion | bytes 9216 | tf_op jit(solution)/shard_map/jit(_take)/gather | solution.py:46
  287.3 0.0 slice-start
  287.4 0.0 copy-start.5
  287.4 4.5 %gather_fusion.3 = bf16[768,32,128]{2,1,0:T(8,128)(2,1)} fusion(bf16[256,32,128]{2,1,0:T(8,128)(2,1)S(1)} %copy-done, s32[1024]{0:T(1024)S(1)} %pad_clamp_fusion.3), kind=kCustom, calls=%fused_computation.3 | custom fusion | bytes 12585984 | tf_op jit(solution)/shard_map/jit(_take)/gather | solution.py:43
  291.9 0.1 fusion.19
  292.0 0.2 broadcast_compare_fusion
  292.2 0.0 all-gather.2.cloned.1.call-done
  292.3 17.0 %convolution_reduce_fusion = f32[32768]{0:T(1024)S(1)} fusion(bf16[32768,128]{1,0:T(8,128)(2,1)} %bitcast.43, bf16[768,128]{1,0:T(8,128)(2,1)S(1)} %copy-done.5), kind=kOutput, calls=%fused_computation.8 | convolution fusion | flops 6467584000 | bytes 8716288 | tf_op jit(solution)/shard_map/rd,cd->rc/dot_general | solution.py:23
  309.3 0.2 reshape.440
  309.5 0.9 reshape.532
  310.4 6.4 %all-to-all-start = ((f32[64,1,512]{2,1,0:T(1,128)}), f32[64,1,512]{2,1,0:T(1,128)S(1)}, u32[]{:S(2)}, u32[]{:S(2)}) async-start(f32[64,1,512]{2,1,0:T(1,128)} %reshape.532), calls=%async_computation | async-start | bytes 262144 | tf_op jit(solution)/shard_map/all_to_all | solution.py:25
  316.8 0.0 all-reduce.2.cloned.1.call-start
  316.9 8.3 %gather_fusion.2 = bf16[768,32,128]{2,1,0:T(8,128)(2,1)} fusion(bf16[1024,32,128]{2,1,0:T(8,128)(2,1)} %all-gather.2.cloned.1.call-done, s32[1024]{0:T(1024)S(1)} %pad_clamp_fusion.2), kind=kCustom, calls=%fused_computation.2 | custom fusion | bytes 12585984 | tf_op jit(solution)/shard_map/jit(_take)/gather | solution.py:42
  325.2 8.3 %select_reduce_fusion = f32[768,32]{1,0:T(8,128)S(1)} fusion(pred[768,32]{1,0:T(8,128)(4,1)S(1)} %broadcast_compare_fusion, bf16[768,32,128]{2,1,0:T(8,128)(2,1)} %gather_fusion.3, pred[768]{0:T(1024)(128)(4,1)S(1)} %get-tuple-element.9, bf16[768,32,128]{2,1,0:T(8,128)(2,1)} %gather_fusion.2, pred[768]{0:T(1024)(128)(4,1)S(1)} %compare_and_fusion), kind=kOutput, calls=%fused_computation.9 | convolution fusion | flops 209166336 | bytes 12707328 | tf_op jit(solution)/shard_map/ntd,npd->ntp/dot_general | solution.py:44
  333.5 0.1 copy.32
  333.6 0.5 broadcast.518
  334.1 1.0 reduce.8
  335.1 0.2 reshape.533
  335.3 0.1 reduce_max.28
  335.4 0.1 copy.31
  335.4 0.7 pad_maximum_fusion
  336.2 0.0 all-reduce.2.cloned.1.call-update
  336.2 44.7 %all-reduce.2.cloned.1.call-done = f32[784,32]{0,1:T(8,128)} async-done(((f32[784,32]{0,1:T(8,128)}), f32[784,32]{0,1:T(8,128)}) %all-reduce.2.cloned.1.call-update) | async-done | bytes 100368 | tf_op jit(solution)/shard_map/pmax | solution.py:49
  381.0 1.0 slice_reduce_fusion
  382.0 0.7 div.94
  382.7 12.9 %all-to-all-start.1 = ((f32[64,1,12]{2,1,0:T(1,128)}), f32[64,1,12]{2,1,0:T(1,128)S(1)}, u32[]{:S(2)}, u32[]{:S(2)}) async-start(f32[64,1,12]{2,1,0:T(1,128)} %bitcast.9), calls=%async_computation.1 | async-start | bytes 65536 | tf_op jit(solution)/shard_map/all_to_all | solution.py:53
  395.6 0.1 gather.43
  395.7 0.1 reduce_sum.23
  395.7 0.7 slice.37
  396.5 0.7 copy.35
  397.1 7.7 %all-to-all-done.1 = f32[64,1,12]{2,1,0:T(1,128)S(1)} async-done(((f32[64,1,12]{2,1,0:T(1,128)}), f32[64,1,12]{2,1,0:T(1,128)S(1)}, u32[]{:S(2)}, u32[]{:S(2)}) %all-to-all-start.1) | async-done | bytes 3104 | tf_op jit(solution)/shard_map/all_to_all | solution.py:53
  404.9 0.5 broadcast.515
  405.4 0.7 reduce.7
  406.1 0.1 reshape.449
  406.2 1.4 gather_fusion.5
  407.6 0.1 gather.47
  407.7 0.6 and_select_fusion.2
  (32 shorter events, 0.3 us)
Async XLA Ops:
  7.2 280.2 %copy-start = (bf16[256,32,128]{2,1,0:T(8,128)(2,1)S(1)}, bf16[256,32,128]{2,1,0:T(8,128)(2,1)}, u32[]{:S(2)}) copy-start(bf16[256,32,128]{2,1,0:T(8,128)(2,1)} %param.8) | copy-start | bytes 6291460
  7.2 62.1 %copy-start.1 = (s32[16384]{0:T(1024)S(1)}, s32[16384]{0:T(1024)}, u32[]{:S(2)}) copy-start(s32[16384]{0:T(1024)} %param.10) | copy-start | bytes 196612
  7.2 285.1 %all-gather.2.cloned.1.call-start = ((), (), s32[]{:S(2)}) async-start(), calls=%async_computation.2 | async-start | bytes 8519680 | tf_op jit(solution)/shard_map/all_gather | solution.py:20
  69.0 90.8 %copy-start.4 = (s32[64,3]{0,1:T(4,128)}, s32[64,3]{0,1:T(4,128)S(1)}, u32[]{:S(2)}) copy-start(s32[64,3]{0,1:T(4,128)S(1)} %reduce-window.19) | copy-start | bytes 2308
  69.2 213.1 %copy-start.2 = (s32[256]{0:T(256)S(1)}, s32[256]{0:T(256)}, u32[]{:S(2)}) copy-start(s32[256]{0:T(256)} %param.9) | copy-start | bytes 3076
  287.3 4.6 %slice-start = ((s32[64,3]{0,1:T(4,128)}), s32[64,2]{0,1:T(2,128)S(1)}, s32[]{:S(2)}) async-start(s32[64,3]{0,1:T(4,128)} %copy-done.4), calls=%async_computation.4 | async-start | bytes 2048 | tf_op jit(solution)/shard_map/slice.5
  287.4 4.9 %copy-start.5 = (bf16[768,128]{1,0:T(8,128)(2,1)S(1)}, bf16[768,128]{1,0:T(8,128)(2,1)}, u32[]{:S(2)}) copy-start(bf16[768,128]{1,0:T(8,128)(2,1)} %param.7) | copy-start | bytes 589828
  310.4 23.2 %all-to-all-start = ((f32[64,1,512]{2,1,0:T(1,128)}), f32[64,1,512]{2,1,0:T(1,128)S(1)}, u32[]{:S(2)}, u32[]{:S(2)}) async-start(f32[64,1,512]{2,1,0:T(1,128)} %reshape.532), calls=%async_computation | async-start | bytes 262144 | tf_op jit(solution)/shard_map/all_to_all | solution.py:25
  316.8 64.1 %all-reduce.2.cloned.1.call-start = ((), (), s32[]{:S(2)}) async-start(), calls=%async_computation.3 | async-start | bytes 229376 | tf_op jit(solution)/shard_map/pmax | solution.py:49
  325.2 82.5 %copy-start.3 = (s32[16,16]{1,0:T(8,128)S(1)}, s32[16,16]{1,0:T(8,128)}, u32[]{:S(2)}) copy-start(s32[16,16]{1,0:T(8,128)} %param.11) | copy-start | bytes 3076
  382.7 22.2 %all-to-all-start.1 = ((f32[64,1,12]{2,1,0:T(1,128)}), f32[64,1,12]{2,1,0:T(1,128)S(1)}, u32[]{:S(2)}, u32[]{:S(2)}) async-start(f32[64,1,12]{2,1,0:T(1,128)} %bitcast.9), calls=%async_computation.1 | async-start | bytes 65536 | tf_op jit(solution)/shard_map/all_to_all | solution.py:53
Sparse Core Ops, SparseCore 0:
  10.8 87.3 all-gather.1
  336.3 44.5 all-reduce.1
where the time goes:
time: 416 us; the launch traced here: 415 us
  local copies, waits for them, and re-layouts  241 us (58%)
  blocking collectives  55.1 us (13%)
  waiting for transfers between devices  53.2 us (13%)
  matrix products  25.3 us (6%)
  starting transfers between devices  19.4 us (5%)
  between operations  14.4 us (3%)
  other arithmetic  6.63 us (2%)
    gather x1, local copies, waits for them, and re-layouts, per_device(): all_rows = jnp.take(passage_row, cand_block.reshape(-1), axis=0)  90.5 us
    scatter x1, local copies, waits for them, and re-layouts, per_device(): slot_table = jnp.zeros((shard_total * capacity,), jnp.int32).at[places].s...  60.5 us
    scatter x1, local copies, waits for them, and re-layouts, per_device(): jnp.zeros((shard_total * capacity,), jnp.int32).at[places]  60.3 us
    all_gather x1, blocking collectives, per_device(): cand_block = lax.all_gather(candidates, 'shard', axis=0, tiled=True)  55.1 us
    pmax x1, waiting for transfers between devices, per_device(): lax.pmax(jnp.concatenate([shard_best, partial_value], axis=0), 'cent')  44.7 us
    dot_general x1, matrix products, per_device(): jnp.einsum('rd,cd->rc', flattened, centroids, preferred_element_type=jnp....  17 us
    all_to_all x1, starting transfers between devices, per_device(): lax.all_to_all(pair_scores, 'shard', split_axis=0, concat_axis=0, tiled=T...  12.9 us
  transfers between devices with their start and end apart: 4, of which 2 were waited for; matrix products, arithmetic and copies ran while one was open for 60% of the time, Pallas kernels for 0%

commit v1 on v0

--- a/solution.py
+++ b/solution.py
@@ -18,7 +18,9 @@
     pairs_here = query_count * per_query
     my_shard = lax.axis_index("shard")
     query_block = lax.all_gather(queries, "shard", axis=0, tiled=True)
-    cand_block = lax.all_gather(candidates, "shard", axis=0, tiled=True)
+    cand_block = jnp.concatenate(
+        lax.all_to_all(jnp.stack([candidates] * lax.axis_size("shard")), "shard", 0, 0), axis=0
+    )
     flattened = query_block.reshape(-1, feature_width)
     scored = jnp.einsum("rd,cd->rc", flattened, centroids, preferred_element_type=jnp.float32)
     local_best = jnp.max(scored, axis=1).reshape(shard_total, query_count, query_tokens)

time: 416 us -> 381 us (0.916)
  blocking collectives: 55.1 us -> 0 us
  starting transfers between devices: 19.4 us -> 32.3 us
  waiting for transfers between devices: 53.2 us -> 57.4 us
    all_gather x1 -> x0, blocking collectives: 55.1 us -> none  [per_device(): cand_block = lax.all_gather(candidates, 'shard', axis=0, tiled=True)]
    all_to_all x0 -> x1, starting transfers between devices: none -> 13.1 us  [per_device(): lax.all_to_all(jnp.stack([candidates] * lax.axis_size('shard')), 'shard',...]
  transfers between devices with their start and end apart: 4 -> 5, of which waited for: 2 -> 3; matrix products, arithmetic and copies ran while one was open for 60% -> 66% of each run, Pallas kernels for 0% -> 0%
where the time goes in v1:
time: 381 us; the launch traced here: 380 us
  local copies, waits for them, and re-layouts  243 us (64%)
  waiting for transfers between devices  57.4 us (15%)
  starting transfers between devices  32.3 us (8%)
  matrix products  25.3 us (7%)
  between operations  14.4 us (4%)
  other arithmetic  7.43 us (2%)
    gather x1, local copies, waits for them, and re-layouts, per_device(): all_rows = jnp.take(passage_row, cand_block.reshape(-1), axis=0)  90.5 us
    scatter x1, local copies, waits for them, and re-layouts, per_device(): slot_table = jnp.zeros((shard_total * capacity,), jnp.int32).at[places].s...  60.5 us
    scatter x1, local copies, waits for them, and re-layouts, per_device(): jnp.zeros((shard_total * capacity,), jnp.int32).at[places]  60.3 us
    pmax x1, waiting for transfers between devices, per_device(): lax.pmax(jnp.concatenate([shard_best, partial_value], axis=0), 'cent')  44.7 us
    dot_general x1, matrix products, per_device(): jnp.einsum('rd,cd->rc', flattened, centroids, preferred_element_type=jnp....  17 us
    all_to_all x1, starting transfers between devices, per_device(): lax.all_to_all(jnp.stack([candidates] * lax.axis_size('shard')), 'shard',...  13.1 us
    all_to_all x1, starting transfers between devices, per_device(): lax.all_to_all(pair_scores, 'shard', split_axis=0, concat_axis=0, tiled=T...  12.9 us
    gather x1, local copies, waits for them, and re-layouts, per_device(): asked = jnp.take(query_block, query_table, axis=0)  8.3 us
  transfers between devices with their start and end apart: 5, of which 3 were waited for; matrix products, arithmetic and copies ran while one was open for 66% of the time, Pallas kernels for 0%

profile of v1, /device:TPU:1, one launch (start us, length us, event | category | flops | bytes accessed | tf_op | source)
XLA Modules:
  0.0 380.3 jit_solution(4466139559782979723)
XLA Ops:
  7.2 0.0 all-gather.2.cloned.1.call-start
  7.2 0.7 all-gather.2.cloned.1.call-update
  7.9 0.7 stack.2
  8.7 0.9 reshape.524
  9.5 13.1 %all-to-all-start.1 = ((s32[64,1,256]{2,1,0:T(1,128)}), s32[64,1,256]{2,1,0:T(1,128)S(1)}, u32[]{:S(2)}, u32[]{:S(2)}) async-start(s32[64,1,256]{2,1,0:T(1,128)} %reshape.524), calls=%async_computation.1 | async-start | bytes 131072 | tf_op jit(solution)/shard_map/all_to_all | solution.py:22
  22.7 0.8 reshape.437
  23.5 0.8 reshape.439
  24.2 0.8 reshape.438
  25.0 2.1 gather_fusion.4
  27.1 0.6 reduce-window.16
  27.8 0.2 slice_reduce_fusion.1
  28.0 0.1 broadcast_bitcast_fusion
  28.1 0.1 copy.41
  28.2 0.1 fusion.19
  28.3 4.2 %all-to-all-done.1 = s32[64,1,256]{2,1,0:T(1,128)S(1)} async-done(((s32[64,1,256]{2,1,0:T(1,128)}), s32[64,1,256]{2,1,0:T(1,128)S(1)}, u32[]{:S(2)}, u32[]{:S(2)}) %all-to-all-start.1) | async-done | bytes 65568 | tf_op jit(solution)/shard_map/all_to_all | solution.py:22
  32.4 0.5 broadcast.520
  32.9 0.8 reduce.8
  33.7 0.2 reshape.525
  33.9 0.2 reshape_reshape.7
  34.2 0.2 reshape_reshape.9
  34.4 0.3 copy.29
  34.6 0.1 compare_select_fusion.1
  34.8 90.5 %gather_fusion = s32[16384]{0:T(1024)S(1)} fusion(s32[16384]{0:T(1024)S(1)} %copy-done.1, s32[16384]{0:T(1024)S(1)} %broadcast_clamp_fusion), kind=kCustom, calls=%fused_computation | custom fusion | bytes 196608 | tf_op jit(solution)/shard_map/jit(_take)/gather | solution.py:29
  125.3 0.1 copy.30
  125.4 0.1 fusion.23
  125.5 0.6 reduce-window.14
  126.1 0.2 slice_reduce_fusion.2
  126.3 0.1 broadcast_add_fusion
  126.4 0.1 copy.34
  126.5 0.5 compare_select_fusion
  127.0 60.3 %scatter_custom_fusion.1 = s32[768]{0:T(1024)S(1)} fusion(s32[16384]{0:T(1024)S(1)} %bitcast.51, s32[16384]{0:T(1024)S(1)} %add_select_fusion, s32[]{:T(128)} %constant.143.clone.1), kind=kCustom, calls=%fused_computation.97 | custom fusion | bytes 3076 | tf_op jit(solution)/shard_map/scatter | solution.py:42
  187.4 60.5 %scatter_custom_fusion = s32[768]{0:T(1024)S(1)} fusion(s32[16384]{0:T(1024)S(1)} %bitcast.52, s32[16384]{0:T(1024)S(1)} %add_select_fusion.1, s32[]{:T(128)} %constant.143.clone.1), kind=kCustom, calls=%fused_computation.99 | custom fusion | bytes 3076 | tf_op jit(solution)/shard_map/scatter | solution.py:39
  247.9 5.0 %gather_fusion.1 = s32[768]{0:T(1024)S(1)} fusion(s32[256]{0:T(256)S(1)} %copy-done.2, s32[1024]{0:T(1024)S(1)} %pad_clamp_fusion.3), kind=kCustom, calls=%fused_computation.1 | custom fusion | bytes 9216 | tf_op jit(solution)/shard_map/jit(_take)/gather | solution.py:48
  252.9 4.5 %gather_fusion.3 = bf16[768,32,128]{2,1,0:T(8,128)(2,1)} fusion(bf16[256,32,128]{2,1,0:T(8,128)(2,1)S(1)} %copy-done, s32[1024]{0:T(1024)S(1)} %pad_clamp_fusion.3), kind=kCustom, calls=%fused_computation.3 | custom fusion | bytes 12585984 | tf_op jit(solution)/shard_map/jit(_take)/gather | solution.py:45
  257.5 0.2 broadcast_compare_fusion
  257.7 17.0 %convolution_reduce_fusion = f32[32768]{0:T(1024)S(1)} fusion(bf16[32768,128]{1,0:T(8,128)(2,1)} %bitcast.44, bf16[768,128]{1,0:T(8,128)(2,1)S(1)} %copy-done.4), kind=kOutput, calls=%fused_computation.8 | convolution fusion | flops 6467584000 | bytes 8716288 | tf_op jit(solution)/shard_map/rd,cd->rc/dot_general | solution.py:25
  274.7 0.2 reshape.435
  274.9 0.9 reshape.526
  275.8 6.2 %all-to-all-start = ((f32[64,1,512]{2,1,0:T(1,128)}), f32[64,1,512]{2,1,0:T(1,128)S(1)}, u32[]{:S(2)}, u32[]{:S(2)}) async-start(f32[64,1,512]{2,1,0:T(1,128)} %reshape.526), calls=%async_computation | async-start | bytes 262144 | tf_op jit(solution)/shard_map/all_to_all | solution.py:27
  282.0 0.0 all-reduce.2.cloned.1.call-start
  282.0 8.3 %gather_fusion.2 = bf16[768,32,128]{2,1,0:T(8,128)(2,1)} fusion(bf16[1024,32,128]{2,1,0:T(8,128)(2,1)} %all-gather.2.cloned.1.call-done, s32[1024]{0:T(1024)S(1)} %pad_clamp_fusion.2), kind=kCustom, calls=%fused_computation.2 | custom fusion | bytes 12585984 | tf_op jit(solution)/shard_map/jit(_take)/gather | solution.py:44
  290.3 8.3 %select_reduce_fusion = f32[768,32]{1,0:T(8,128)S(1)} fusion(pred[768,32]{1,0:T(8,128)(4,1)S(1)} %broadcast_compare_fusion, bf16[768,32,128]{2,1,0:T(8,128)(2,1)} %gather_fusion.3, pred[768]{0:T(1024)(128)(4,1)S(1)} %get-tuple-element.9, bf16[768,32,128]{2,1,0:T(8,128)(2,1)} %gather_fusion.2, pred[768]{0:T(1024)(128)(4,1)S(1)} %compare_and_fusion), kind=kOutput, calls=%fused_computation.9 | convolution fusion | flops 209166336 | bytes 12707328 | tf_op jit(solution)/shard_map/ntd,npd->ntp/dot_general | solution.py:46
  298.6 0.1 copy.36
  298.8 0.5 broadcast.521
  299.3 1.0 reduce.9
  300.2 0.2 reshape.527
  300.4 0.1 reduce_max.28
  300.5 0.1 copy.35
  300.6 0.7 pad_maximum_fusion
  301.4 44.7 %all-reduce.2.cloned.1.call-done = f32[784,32]{0,1:T(8,128)} async-done(((f32[784,32]{0,1:T(8,128)}), f32[784,32]{0,1:T(8,128)}) %all-reduce.2.cloned.1.call-update) | async-done | bytes 100368 | tf_op jit(solution)/shard_map/pmax | solution.py:51
  346.1 1.0 slice_reduce_fusion
  347.1 0.7 div.94
  347.8 12.9 %all-to-all-start.2 = ((f32[64,1,12]{2,1,0:T(1,128)}), f32[64,1,12]{2,1,0:T(1,128)S(1)}, u32[]{:S(2)}, u32[]{:S(2)}) async-start(f32[64,1,12]{2,1,0:T(1,128)} %bitcast.10), calls=%async_computation.2 | async-start | bytes 65536 | tf_op jit(solution)/shard_map/all_to_all | solution.py:55
  360.7 0.1 gather.43
  360.8 0.1 reduce_sum.23
  360.9 0.7 slice.37
  361.6 0.7 copy.39
  362.3 7.7 %all-to-all-done.2 = f32[64,1,12]{2,1,0:T(1,128)S(1)} async-done(((f32[64,1,12]{2,1,0:T(1,128)}), f32[64,1,12]{2,1,0:T(1,128)S(1)}, u32[]{:S(2)}, u32[]{:S(2)}) %all-to-all-start.2) | async-done | bytes 3104 | tf_op jit(solution)/shard_map/all_to_all | solution.py:55
  370.0 0.5 broadcast.517
  370.5 0.7 reduce.7
  371.3 0.1 reshape.441
  371.4 1.4 gather_fusion.5
  372.8 0.1 gather.47
  372.8 0.6 and_select_fusion.2
  (36 shorter events, 0.3 us)
Async XLA Ops:
  7.2 245.7 %copy-start = (bf16[256,32,128]{2,1,0:T(8,128)(2,1)S(1)}, bf16[256,32,128]{2,1,0:T(8,128)(2,1)}, u32[]{:S(2)}) copy-start(bf16[256,32,128]{2,1,0:T(8,128)(2,1)} %param.8) | copy-start | bytes 6291460
  7.2 27.6 %copy-start.1 = (s32[16384]{0:T(1024)S(1)}, s32[16384]{0:T(1024)}, u32[]{:S(2)}) copy-start(s32[16384]{0:T(1024)} %param.10) | copy-start | bytes 196612
  7.2 250.5 %all-gather.2.cloned.1.call-start = ((), (), s32[]{:S(2)}) async-start(), calls=%async_computation.3 | async-start | bytes 8519680 | tf_op jit(solution)/shard_map/all_gather | solution.py:20
  9.5 22.9 %all-to-all-start.1 = ((s32[64,1,256]{2,1,0:T(1,128)}), s32[64,1,256]{2,1,0:T(1,128)S(1)}, u32[]{:S(2)}, u32[]{:S(2)}) async-start(s32[64,1,256]{2,1,0:T(1,128)} %reshape.524), calls=%async_computation.1 | async-start | bytes 131072 | tf_op jit(solution)/shard_map/all_to_all | solution.py:22
  34.7 213.1 %copy-start.2 = (s32[256]{0:T(256)S(1)}, s32[256]{0:T(256)}, u32[]{:S(2)}) copy-start(s32[256]{0:T(256)} %param.9) | copy-start | bytes 3076
  252.9 4.8 %copy-start.4 = (bf16[768,128]{1,0:T(8,128)(2,1)S(1)}, bf16[768,128]{1,0:T(8,128)(2,1)}, u32[]{:S(2)}) copy-start(bf16[768,128]{1,0:T(8,128)(2,1)} %param.7) | copy-start | bytes 589828
  275.8 23.0 %all-to-all-start = ((f32[64,1,512]{2,1,0:T(1,128)}), f32[64,1,512]{2,1,0:T(1,128)S(1)}, u32[]{:S(2)}, u32[]{:S(2)}) async-start(f32[64,1,512]{2,1,0:T(1,128)} %reshape.526), calls=%async_computation | async-start | bytes 262144 | tf_op jit(solution)/shard_map/all_to_all | solution.py:27
  282.0 64.1 %all-reduce.2.cloned.1.call-start = ((), (), s32[]{:S(2)}) async-start(), calls=%async_computation.4 | async-start | bytes 229376 | tf_op jit(solution)/shard_map/pmax | solution.py:51
  290.3 82.5 %copy-start.3 = (s32[16,16]{1,0:T(8,128)S(1)}, s32[16,16]{1,0:T(8,128)}, u32[]{:S(2)}) copy-start(s32[16,16]{1,0:T(8,128)} %param.11) | copy-start | bytes 3076
  347.8 22.2 %all-to-all-start.2 = ((f32[64,1,12]{2,1,0:T(1,128)}), f32[64,1,12]{2,1,0:T(1,128)S(1)}, u32[]{:S(2)}, u32[]{:S(2)}) async-start(f32[64,1,12]{2,1,0:T(1,128)} %bitcast.10), calls=%async_computation.2 | async-start | bytes 65536 | tf_op jit(solution)/shard_map/all_to_all | solution.py:55
Sparse Core Ops, SparseCore 0:
  10.8 87.2 all-gather.1
  301.5 44.5 all-reduce.1
